TPU v7x, 256 devices: a whole 4x4x8 slice. The times are simulated.
256 devices in a mesh: dp: 32 (over x_lo, z, core), blk: 8 (over y, x_hi).
Axes of the slice: x: 4 (x_hi: 2, x_lo: 2; x = x_hi * 2 + x_lo), y: 4, z: 8, core: 2. Of those that a mesh axis runs over, the one named last changes fastest.
Arguments:
- inputs: bfloat16 [8, 16384, 4096], P('blk', 'dp'), may hold values from -6 to 6
- out_grads: bfloat16 [8, 16384, 4096], P('blk', 'dp'), may hold values from -8 to 8
- test_matrix: bfloat16 [8, 4096, 256], P('blk'), may hold values from -6 to 6
- momentum: bfloat16 [8, 4096, 4096], P(None, 'blk', 'dp'), may hold values from -6 to 6
Outputs:
- update: bfloat16 [8, 4096, 4096], P(None, 'blk', 'dp')
All inputs are finite; a program needn't handle non-finite values.
Results may differ from a plain program's by a relative error of at most 0.0035.
Values may be sent and summed in bfloat16 or wider, within the bound.
No kernel may reach another device: no remote copies, remote signals or barrier semaphores. Data moves between devices by JAX's collectives and lax.ppermute only.
A program may use at most 128 MiB of HBM per device.

v0:
```python
import jax
import jax.numpy as jnp
from jax import lax
from jax.sharding import Mesh
from jax.sharding import PartitionSpec as P

DP = ("dp_0", "dp_1", "dp_2")


def filled_up(lines, devices):
    spare = -len(lines) % devices
    return jnp.pad(lines, [(0, spare)] + [(0, 0)] * (lines.ndim - 1))


def copy_for_each(x, axis):
    devices = lax.axis_size(axis)
    return lax.all_to_all(jnp.broadcast_to(x[None], (devices, *x.shape)), axis, 0, 0, tiled=True)


def in_order(blocks, dim):
    blocks = jnp.moveaxis(blocks, 0, dim)
    lengths = blocks.shape
    return blocks.reshape(*lengths[:dim], lengths[dim] * lengths[dim + 1], *lengths[dim + 2 :])


def whole_of(x, axes, dim):
    far, near = axes
    first = copy_for_each(x, far)
    blocks = jnp.swapaxes(copy_for_each(first, near), 0, 1)
    return in_order(blocks.reshape(-1, *x.shape), dim)


def in_blocks(x, dim, devices):
    lengths = x.shape
    blocks = x.reshape(*lengths[:dim], devices, lengths[dim] // devices, *lengths[dim + 1 :])
    return jnp.moveaxis(blocks, dim, 0)


def sum_at_owner(x, axis, dim):
    blocks = in_blocks(x, dim, lax.axis_size(axis))
    arrived = lax.all_to_all(blocks, axis, split_axis=0, concat_axis=0, tiled=True)
    return arrived.sum(axis=0)


def sum_by_axis(x, axes, dim):
    far, near = axes
    blocks = in_blocks(x, dim, lax.axis_size(far))
    nearer = sum_at_owner(blocks, near, dim + 1)
    arrived = lax.all_to_all(nearer, far, split_axis=0, concat_axis=0, tiled=True)
    return arrived.sum(axis=0)


def total_of(x, axes):
    lines = x.reshape(-1, x.shape[-1])
    padded = filled_up(lines, lax.axis_size(axes[0]) * lax.axis_size(axes[1]))
    whole = whole_of(sum_by_axis(padded, axes, 0), axes, 0)
    return lax.slice_in_dim(whole, 0, len(lines)).reshape(x.shape)


def collect(x, axis, dim):
    blocks = copy_for_each(x, axis)
    return in_order(blocks, dim)


def total_of_2(x, axes):
    lines = x.reshape(-1, x.shape[-1])
    own = sum_at_owner(filled_up(lines, lax.axis_size(axes)), axes, 0)
    whole = collect(own, axes, 0)
    return whole[: len(lines)].reshape(x.shape)


def inner_gram(columns):
    return lax.dot_general(
        columns, columns, (((0,), (0,)), ((), ())), precision=lax.Precision.HIGHEST
    )


def cholesky_pass(columns, gram_matrix):
    lower_factor = jnp.linalg.cholesky(gram_matrix)
    return lax.linalg.triangular_solve(
        lower_factor, columns, left_side=False, lower=True, transpose_a=True
    )


def shards(inputs, out_grads, test_matrix, momentum):
    features = inputs[0]
    errors = out_grads[0]
    probes = test_matrix[0]
    replicas = lax.axis_size(DP)
    scale = 1.0 / (features.shape[1] * features.shape[0] * replicas)
    projected = jnp.dot(features, probes, preferred_element_type=jnp.float32).astype(jnp.bfloat16)
    token_gram = lax.dot_general(
        errors, errors, (((1,), (1,)), ((), ())), preferred_element_type=jnp.float32
    ).astype(jnp.bfloat16)
    mixed_rows = jnp.dot(token_gram, projected, preferred_element_type=jnp.float32).astype(
        jnp.bfloat16
    )
    sketch_term = (
        lax.dot_general(
            features, mixed_rows, (((0,), (0,)), ((), ())), preferred_element_type=jnp.float32
        )
        * scale
    )
    sketch = total_of(sketch_term, (("dp_0", "dp_1"), "dp_2"))
    basis = cholesky_pass(sketch, inner_gram(sketch)).astype(jnp.bfloat16)
    reduced = jnp.dot(features, basis, preferred_element_type=jnp.float32).astype(jnp.bfloat16)
    shaped = jnp.dot(token_gram, reduced, preferred_element_type=jnp.float32).astype(jnp.bfloat16)
    core_term = (
        lax.dot_general(
            reduced, shaped, (((0,), (0,)), ((), ())), preferred_element_type=jnp.float32
        )
        * scale
    )
    core_matrix = total_of_2(core_term, DP)
    shifted = core_matrix + jnp.eye(core_matrix.shape[0], dtype=jnp.float32)
    lower_factor = jnp.linalg.cholesky(shifted)
    half_solved = lax.linalg.triangular_solve(lower_factor, core_matrix, left_side=True, lower=True)
    factor = lax.linalg.triangular_solve(
        lower_factor, half_solved, left_side=True, lower=True, transpose_a=True
    )
    columns = lax.all_to_all(momentum, "blk", split_axis=0, concat_axis=1, tiled=True)[0]
    coeffs = lax.dot_general(
        basis, columns, (((0,), (0,)), ((), ())), preferred_element_type=jnp.float32
    )
    scaled = jnp.dot(factor, coeffs, precision=lax.Precision.HIGHEST).astype(jnp.bfloat16)
    fresh = (
        columns.astype(jnp.float32) - jnp.dot(basis, scaled, preferred_element_type=jnp.float32)
    ).astype(jnp.bfloat16)
    return lax.all_to_all(fresh[None], "blk", split_axis=1, concat_axis=0, tiled=True)


def solution(mesh):
    torus = Mesh(mesh.devices.reshape(2, 8, 2, mesh.shape["blk"]), ("dp_0", "dp_1", "dp_2", "blk"))
    in_specs = (P("blk", DP, None), P("blk", DP, None), P("blk", None, None), P(None, "blk", DP))
    out_specs = P(None, "blk", DP)
    return jax.shard_map(
        shards, mesh=torus, in_specs=in_specs, out_specs=out_specs, check_vma=False
    )
```

profile of v0, /device:TPU:1, one launch (start us, length us, event | category | flops | bytes accessed | tf_op | source)
XLA Modules:
  0.0 433.6 jit_solution(7566562634158218286)
XLA Ops:
  0.0 6.0 %fusion.16 = bf16[512,512]{1,0:T(8,128)(2,1)S(1)} fusion(bf16[1,512,4096]{2,1,0:T(8,128)(2,1)} %param.6), kind=kOutput, calls=%fused_computation.26 | convolution fusion | flops 2147745792 | bytes 4718592 | tf_op jit(solution)/shard_map/dot_general | solution.py:92
  13.2 6.6 %reshape_reshape.6 = f32[16,2,128,256]{2,1,0,3:T(2,128)} reshape(f32[4096,256]{0,1:T(8,128)} %fusion) | data formatting | bytes 8388608 | tf_op jit(solution)/shard_map/reshape;reshape | solution.py:35
  24.2 8.8 %all-to-all-start.1 = ((f32[2,16,128,256]{2,1,3,0:T(8,128)}), f32[2,16,128,256]{2,1,3,0:T(8,128)}, u32[]{:S(2)}, u32[]{:S(2)}) async-start(f32[2,16,128,256]{2,1,3,0:T(8,128)} %bitcast.138), calls=%async_computation.1 | async-start | bytes 8388608 | tf_op jit(solution)/shard_map/all_to_all | solution.py:41
  40.6 54.2 %all_to_all.54 = f32[16,128,256]{1,2,0:T(8,128)S(1)} all-to-all(f32[16,128,256]{1,2,0:T(8,128)S(1)} %copy.30), channel_id=1, replica_groups=mesh['dp_0'=2,'dp_1'=8,'dp_2'=2,'blk'=8] {'dp_0','dp_1'}, dimensions={0} | all-to-all | bytes 4194304 | tf_op jit(solution)/shard_map/all_to_all | solution.py:49
  96.6 7.1 %all-to-all-start.3 = ((f32[16,128,256]{2,1,0:T(8,128)}), f32[16,128,256]{2,1,0:T(8,128)S(1)}, u32[]{:S(2)}, u32[]{:S(2)}) async-start(f32[16,128,256]{2,1,0:T(8,128)} %broadcast_in_dim.8), calls=%async_computation.3 | async-start | bytes 4194304 | tf_op jit(solution)/shard_map/all_to_all | solution.py:17
  103.7 47.7 %all-to-all-done.3 = f32[16,128,256]{2,1,0:T(8,128)S(1)} async-done(((f32[16,128,256]{2,1,0:T(8,128)}), f32[16,128,256]{2,1,0:T(8,128)S(1)}, u32[]{:S(2)}, u32[]{:S(2)}) %all-to-all-start.3) | async-done | bytes 2097184 | tf_op jit(solution)/shard_map/all_to_all | solution.py:17
  151.9 8.8 %all_to_all.51 = f32[2,16,128,256]{3,2,1,0:T(8,128)S(1)} all-to-all(f32[2,16,128,256]{3,2,1,0:T(8,128)S(1)} %broadcast_in_dim.10), channel_id=1, replica_groups=mesh['dp_0'=2,'dp_1'=8,'dp_2'=2,'blk'=8] {'dp_2'}, dimensions={0} | all-to-all | bytes 8388608 | tf_op jit(solution)/shard_map/all_to_all | solution.py:17
  162.6 6.8 %fusion.28 = f32[256,256]{1,0:T(8,128)S(1)} fusion(f32[2,16,128,256]{3,2,1,0:T(8,128)S(1)} %all_to_all.51), kind=kOutput, calls=%fused_computation.32 | convolution fusion | flops 3221225472 | bytes 4456448 | tf_op jit(solution)/shard_map/dot_general | solution.py:73
  169.6 11.7 %cholesky.130 = f32[128,128]{1,0:T(8,128)S(1)} custom-call(f32[128,128]{1,0:T(8,128)S(1)} %cholesky.194), custom_call_target="Cholesky" | custom-call | tf_op jit(solution)/shard_map/jit(cholesky)/cholesky | solution.py:79
  181.4 10.2 %custom-call.19 = f32[1,128,128]{1,2,0:T(8,128)S(1)} custom-call(f32[1,128,128]{2,1,0:T(8,128)S(1)} %get-tuple-element.49), custom_call_target="InvertDiagBlocksLowerTriangular" | custom-call | tf_op jit(solution)/shard_map/jit(cholesky)/cholesky | solution.py:79
  192.1 11.7 %cholesky.147 = f32[128,128]{1,0:T(8,128)S(1)} custom-call(f32[128,128]{1,0:T(8,128)S(1)} %convolution_subtract_fusion.5), custom_call_target="Cholesky" | custom-call | tf_op jit(solution)/shard_map/jit(cholesky)/cholesky | solution.py:79
  210.1 19.8 %custom-call.16 = f32[2,128,128]{1,2,0:T(8,128)S(1)} custom-call(f32[2,128,128]{2,1,0:T(8,128)S(1)} %get-tuple-element.13), custom_call_target="InvertDiagBlocksLowerTriangular" | custom-call | tf_op jit(solution)/shard_map/triangular_solve | solution.py:80
  243.0 17.9 %all_to_all.52 = f32[32,8,256]{2,1,0:T(8,128)S(1)} all-to-all(f32[32,8,256]{2,1,0:T(8,128)S(1)} %fusion.34), channel_id=1, replica_groups=mesh['dp_0'=2,'dp_1'=8,'dp_2'=2,'blk'=8] {'dp_0','dp_1','dp_2'}, dimensions={0} | all-to-all | bytes 524288 | tf_op jit(solution)/shard_map/all_to_all | solution.py:41
  260.9 6.4 %all-to-all-start = ((bf16[8,512,128]{2,1,0:T(8,128)(2,1)}), bf16[8,512,128]{2,1,0:T(8,128)(2,1)S(1)}, u32[]{:S(2)}, u32[]{:S(2)}) async-start(bf16[8,512,128]{2,1,0:T(8,128)(2,1)} %param.8), calls=%async_computation | async-start | bytes 2097152 | tf_op jit(solution)/shard_map/all_to_all | solution.py:121
  267.3 15.1 %all-to-all-done = bf16[8,512,128]{2,1,0:T(8,128)(2,1)S(1)} async-done(((bf16[8,512,128]{2,1,0:T(8,128)(2,1)}), bf16[8,512,128]{2,1,0:T(8,128)(2,1)S(1)}, u32[]{:S(2)}, u32[]{:S(2)}) %all-to-all-start) | async-done | bytes 1048608 | tf_op jit(solution)/shard_map/all_to_all | solution.py:121
  283.2 6.8 %all-to-all-start.6 = ((f32[32,8,256]{2,1,0:T(8,128)}), f32[32,8,256]{2,1,0:T(8,128)S(1)}, u32[]{:S(2)}, u32[]{:S(2)}) async-start(f32[32,8,256]{2,1,0:T(8,128)} %broadcast_in_dim.11), calls=%async_computation.6 | async-start | bytes 524288 | tf_op jit(solution)/shard_map/all_to_all | solution.py:17
  291.9 10.0 %all-to-all-done.6 = f32[32,8,256]{2,1,0:T(8,128)S(1)} async-done(((f32[32,8,256]{2,1,0:T(8,128)}), f32[32,8,256]{2,1,0:T(8,128)S(1)}, u32[]{:S(2)}, u32[]{:S(2)}) %all-to-all-start.6) | async-done | bytes 262176 | tf_op jit(solution)/shard_map/all_to_all | solution.py:17
  302.3 11.7 %cholesky.164 = f32[128,128]{1,0:T(8,128)S(1)} custom-call(f32[128,128]{1,0:T(8,128)S(1)} %cholesky.197), custom_call_target="Cholesky" | custom-call | tf_op jit(solution)/shard_map/jit(cholesky)/cholesky | solution.py:116
  314.1 9.8 %custom-call.20 = f32[1,128,128]{1,2,0:T(8,128)S(1)} custom-call(f32[1,128,128]{2,1,0:T(8,128)S(1)} %get-tuple-element.45), custom_call_target="InvertDiagBlocksLowerTriangular" | custom-call | tf_op jit(solution)/shard_map/jit(cholesky)/cholesky | solution.py:116
  324.4 11.7 %cholesky.181 = f32[128,128]{1,0:T(8,128)S(1)} custom-call(f32[128,128]{1,0:T(8,128)S(1)} %convolution_subtract_fusion.4), custom_call_target="Cholesky" | custom-call | tf_op jit(solution)/shard_map/jit(cholesky)/cholesky | solution.py:116
  343.0 19.9 %custom-call.17 = f32[2,128,128]{1,2,0:T(8,128)S(1)} custom-call(f32[2,128,128]{2,1,0:T(8,128)S(1)} %get-tuple-element.21), custom_call_target="InvertDiagBlocksLowerTriangular" | custom-call | tf_op jit(solution)/shard_map/triangular_solve | solution.py:118
  367.0 16.7 %copy.57 = bf16[1,4096,128]{2,0,1:T(2,128)(2,1)S(1)} copy(bf16[1,4096,128]{2,1,0:T(8,128)(2,1)S(1)} %fusion.2) | data formatting | bytes 2097152 | tf_op jit(solution)/shard_map/broadcast_in_dim | solution.py:129
  384.3 22.4 %reduce.8 = bf16[4096,128]{1,0:T(8,128)(2,1)S(1)} reduce(bf16[4096,1,128]{2,1,0:T(2,128)(2,1)S(1)} %bitcast.142, bf16[]{:T(256)} %broadcast.130), dimensions={1}, to_apply=%bitcast.125.reduce_sub_computation | reduce | bytes 2097154
  407.8 19.2 %all_to_all.53 = bf16[8,2,32768]{2,1,0:T(2,128)(2,1)S(1)} all-to-all(bf16[8,2,32768]{2,1,0:T(2,128)(2,1)} %reshape.82), channel_id=1, replica_groups=mesh['dp_0'=2,'dp_1'=8,'dp_2'=2,'blk'=8] {'blk'}, dimensions={0} | all-to-all | bytes 2097152 | tf_op jit(solution)/shard_map/all_to_all | solution.py:129
  (88 shorter events, 71.0 us)
Async XLA Ops:
  0.0 6.0 %copy-start = (bf16[1,4096,256]{2,1,0:T(8,128)(2,1)S(1)}, bf16[1,4096,256]{2,1,0:T(8,128)(2,1)}, u32[]{:S(2)}) copy-start(bf16[1,4096,256]{2,1,0:T(8,128)(2,1)} %param.7) | copy-start | bytes 6291460
  0.0 6.0 %copy-start.3 = (bf16[1,512,4096]{2,1,0:T(8,128)(2,1)S(1)}, bf16[1,512,4096]{2,1,0:T(8,128)(2,1)}, u32[]{:S(2)}) copy-start(bf16[1,512,4096]{2,1,0:T(8,128)(2,1)} %param.5) | copy-start | bytes 12582916
  24.2 13.0 %all-to-all-start.1 = ((f32[2,16,128,256]{2,1,3,0:T(8,128)}), f32[2,16,128,256]{2,1,3,0:T(8,128)}, u32[]{:S(2)}, u32[]{:S(2)}) async-start(f32[2,16,128,256]{2,1,3,0:T(8,128)} %bitcast.138), calls=%async_computation.1 | async-start | bytes 8388608 | tf_op jit(solution)/shard_map/all_to_all | solution.py:41
  96.6 54.8 %all-to-all-start.3 = ((f32[16,128,256]{2,1,0:T(8,128)}), f32[16,128,256]{2,1,0:T(8,128)S(1)}, u32[]{:S(2)}, u32[]{:S(2)}) async-start(f32[16,128,256]{2,1,0:T(8,128)} %broadcast_in_dim.8), calls=%async_computation.3 | async-start | bytes 4194304 | tf_op jit(solution)/shard_map/all_to_all | solution.py:17
  160.7 1.9 copy-start.2
  234.5 5.6 %copy-start.7 = (bf16[4096,128]{0,1:T(8,128)(2,1)}, bf16[4096,128]{0,1:T(8,128)(2,1)S(1)}, u32[]{:S(2)}) copy-start(bf16[4096,128]{0,1:T(8,128)(2,1)S(1)} %get-tuple-element.52) | copy-start | bytes 3145732
  234.5 6.6 %copy-start.4 = (bf16[1,512,4096]{2,1,0:T(8,128)(2,1)S(1)}, bf16[1,512,4096]{2,1,0:T(8,128)(2,1)}, u32[]{:S(2)}) copy-start(bf16[1,512,4096]{2,1,0:T(8,128)(2,1)} %param.5) | copy-start | bytes 12582916
  240.1 1.0 copy-start.5
  242.4 47.6 %copy-start.6 = (bf16[4096,128]{0,1:T(8,128)(2,1)S(1)}, bf16[4096,128]{0,1:T(8,128)(2,1)}, u32[]{:S(2)}) copy-start(bf16[4096,128]{0,1:T(8,128)(2,1)} %copy-done.5) | copy-start | bytes 3145732
  260.9 21.5 %all-to-all-start = ((bf16[8,512,128]{2,1,0:T(8,128)(2,1)}), bf16[8,512,128]{2,1,0:T(8,128)(2,1)S(1)}, u32[]{:S(2)}, u32[]{:S(2)}) async-start(bf16[8,512,128]{2,1,0:T(8,128)(2,1)} %param.8), calls=%async_computation | async-start | bytes 2097152 | tf_op jit(solution)/shard_map/all_to_all | solution.py:121
  283.2 18.8 %all-to-all-start.6 = ((f32[32,8,256]{2,1,0:T(8,128)}), f32[32,8,256]{2,1,0:T(8,128)S(1)}, u32[]{:S(2)}, u32[]{:S(2)}) async-start(f32[32,8,256]{2,1,0:T(8,128)} %broadcast_in_dim.11), calls=%async_computation.6 | async-start | bytes 524288 | tf_op jit(solution)/shard_map/all_to_all | solution.py:17
  406.7 26.5 %copy-start.1 = (bf16[1,4096,256]{2,1,0:T(8,128)(2,1)S(1)}, bf16[1,4096,256]{2,1,0:T(8,128)(2,1)}, u32[]{:S(2)}) copy-start(bf16[1,4096,256]{2,1,0:T(8,128)(2,1)} %param.7) | copy-start | bytes 6291460
where the time goes:
time: 441 us; the launch traced here: 434 us
  other arithmetic  134 us (30%)
  blocking collectives  100 us (23%)
  waiting for transfers between devices  76.9 us (17%)
  local copies, waits for them, and re-layouts  53.2 us (12%)
  matrix products  36.3 us (8%)
  starting transfers between devices  29.1 us (7%)
    all_to_all x2, waiting for transfers between devices, copy_for_each(): lax.all_to_all(jnp.broadcast_to(x[None], (devices, *x.shape)), axis, 0, 0...  57.7 us
    all_to_all x1, blocking collectives, sum_by_axis(): lax.all_to_all(nearer, far, split_axis=0, concat_axis=0, tiled=True)  54.2 us
    another operation x7, other arithmetic, shards(): lower_factor = jnp.linalg.cholesky(shifted)  34.7 us
    another operation x6, other arithmetic, cholesky_pass(): lower_factor = jnp.linalg.cholesky(gram_matrix)  34.4 us
    unnamed x1, other arithmetic  22.4 us
    another operation x2, other arithmetic, shards(): lax.linalg.triangular_solve(lower_factor, half_solved, left_side=True, lo...  20 us
    another operation x3, other arithmetic, cholesky_pass(): lax.linalg.triangular_solve(lower_factor, columns, left_side=False, lower...  19.9 us
    all_to_all x1, blocking collectives, shards(): lax.all_to_all(fresh[None], 'blk', split_axis=1, concat_axis=0, tiled=True)  19.2 us
  transfers between devices with their start and end apart: 4, of which 4 were waited for; matrix products, arithmetic and copies ran while one was open for 0% of the time, Pallas kernels for 0%

commit v1 on v0

--- a/solution.py
+++ b/solution.py
@@ -3,8 +3,16 @@
 from jax import lax
 from jax.sharding import Mesh
 from jax.sharding import PartitionSpec as P
+from jax.lax import all_to_all, axis_size
 
 DP = ("dp_0", "dp_1", "dp_2")
+
+
+def _meet_targets(u_in, k_dim, out_dim):
+    later = axis_size("blk")
+    kept_arr = jnp.split(u_in, later, axis=k_dim)
+    all_values = all_to_all(jnp.stack(kept_arr), axis_name="blk", split_axis=0, concat_axis=0)
+    return jnp.concatenate(all_values, axis=out_dim)
 
 
 def filled_up(lines, devices):
@@ -126,7 +134,7 @@
     fresh = (
         columns.astype(jnp.float32) - jnp.dot(basis, scaled, preferred_element_type=jnp.float32)
     ).astype(jnp.bfloat16)
-    return lax.all_to_all(fresh[None], "blk", split_axis=1, concat_axis=0, tiled=True)
+    return _meet_targets(fresh[None], 1, 0)
 
 
 def solution(mesh):

time: 441 us -> 394 us (0.89)
  local copies, waits for them, and re-layouts: 53.2 us -> 29.6 us
  other arithmetic: 134 us -> 112 us
    unnamed x1 -> x0, other arithmetic: 22.4 us -> none
    broadcast_in_dim x1 -> x0, local copies, waits for them, and re-layouts: 16.7 us -> none  [shards(): fresh[None]]
    unnamed x22 -> x30, local copies, waits for them, and re-layouts: 10.7 us -> 4.04 us
  transfers between devices with their start and end apart: 4 -> 4, of which waited for: 4 -> 4; matrix products, arithmetic and copies ran while one was open for 0% -> 1% of each run, Pallas kernels for 0% -> 0%
where the time goes in v1:
time: 394 us; the launch traced here: 387 us
  other arithmetic  112 us (28%)
  blocking collectives  99.1 us (25%)
  waiting for transfers between devices  76.9 us (20%)
  matrix products  36.8 us (9%)
  local copies, waits for them, and re-layouts  29.6 us (8%)
  starting transfers between devices  29 us (7%)
    all_to_all x2, waiting for transfers between devices, copy_for_each(): lax.all_to_all(jnp.broadcast_to(x[None], (devices, *x.shape)), axis, 0, 0...  57.7 us
    all_to_all x1, blocking collectives, sum_by_axis(): lax.all_to_all(nearer, far, split_axis=0, concat_axis=0, tiled=True)  54.2 us
    another operation x7, other arithmetic, shards(): lower_factor = jnp.linalg.cholesky(shifted)  34.6 us
    another operation x6, other arithmetic, cholesky_pass(): lower_factor = jnp.linalg.cholesky(gram_matrix)  34.2 us
    another operation x3, other arithmetic, cholesky_pass(): lax.linalg.triangular_solve(lower_factor, columns, left_side=False, lower...  20.1 us
    another operation x2, other arithmetic, shards(): lax.linalg.triangular_solve(lower_factor, half_solved, left_side=True, lo...  19.9 us
    all_to_all x1, blocking collectives, _meet_targets(): all_to_all(jnp.stack(kept_arr), axis_name='blk', split_axis=0, concat_axi...  18.1 us
    all_to_all x1, blocking collectives, sum_at_owner(): lax.all_to_all(blocks, axis, split_axis=0, concat_axis=0, tiled=True)  17.9 us
  transfers between devices with their start and end apart: 4, of which 4 were waited for; matrix products, arithmetic and copies ran while one was open for 1% of the time, Pallas kernels for 0%

profile of v1, /device:TPU:1, one launch (start us, length us, event | category | flops | bytes accessed | tf_op | source)
XLA Modules:
  0.0 386.6 jit_solution(2916420904119000058)
XLA Ops:
  0.0 6.0 %fusion.16 = bf16[512,512]{1,0:T(8,128)(2,1)S(1)} fusion(bf16[1,512,4096]{2,1,0:T(8,128)(2,1)} %param.6), kind=kOutput, calls=%fused_computation.26 | convolution fusion | flops 2147745792 | bytes 4718592 | tf_op jit(solution)/shard_map/dot_general | solution.py:100
  7.3 5.9 %fusion = f32[4096,256]{0,1:T(8,128)} fusion(bf16[1,512,4096]{2,1,0:T(8,128)(2,1)} %param.5, bf16[512,512]{1,0:T(8,128)(2,1)S(1)} %fusion.16, bf16[512,256]{1,0:T(8,128)(2,1)S(1)} %fusion.19), kind=kOutput, calls=%fused_computation.5 | convolution fusion | flops 1209139200 | bytes 9175040 | tf_op jit(solution)/shard_map/dot_general | solution.py:107
  13.2 6.6 %reshape_reshape.6 = f32[16,2,128,256]{2,1,0,3:T(2,128)} reshape(f32[4096,256]{0,1:T(8,128)} %fusion) | data formatting | bytes 8388608 | tf_op jit(solution)/shard_map/reshape;reshape | solution.py:43
  19.8 4.5 %copy.44 = f32[16,2,128,256]{2,0,3,1:T(8,128)} copy(f32[16,2,128,256]{2,1,0,3:T(2,128)} %reshape_reshape.6) | data formatting | bytes 8388608 | tf_op jit(solution)/shard_map/reshape;reshape | solution.py:43
  24.3 8.8 %all-to-all-start.1 = ((f32[2,16,128,256]{2,1,3,0:T(8,128)}), f32[2,16,128,256]{2,1,3,0:T(8,128)}, u32[]{:S(2)}, u32[]{:S(2)}) async-start(f32[2,16,128,256]{2,1,3,0:T(8,128)} %bitcast.166), calls=%async_computation.1 | async-start | bytes 8388608 | tf_op jit(solution)/shard_map/all_to_all | solution.py:49
  40.6 54.2 %all_to_all.47 = f32[16,128,256]{1,2,0:T(8,128)S(1)} all-to-all(f32[16,128,256]{1,2,0:T(8,128)S(1)} %copy.21), channel_id=1, replica_groups=mesh['dp_0'=2,'dp_1'=8,'dp_2'=2,'blk'=8] {'dp_0','dp_1'}, dimensions={0} | all-to-all | bytes 4194304 | tf_op jit(solution)/shard_map/all_to_all | solution.py:57
  96.6 7.1 %all-to-all-start.3 = ((f32[16,128,256]{2,1,0:T(8,128)}), f32[16,128,256]{2,1,0:T(8,128)S(1)}, u32[]{:S(2)}, u32[]{:S(2)}) async-start(f32[16,128,256]{2,1,0:T(8,128)} %broadcast_in_dim.8), calls=%async_computation.3 | async-start | bytes 4194304 | tf_op jit(solution)/shard_map/all_to_all | solution.py:25
  103.7 47.7 %all-to-all-done.3 = f32[16,128,256]{2,1,0:T(8,128)S(1)} async-done(((f32[16,128,256]{2,1,0:T(8,128)}), f32[16,128,256]{2,1,0:T(8,128)S(1)}, u32[]{:S(2)}, u32[]{:S(2)}) %all-to-all-start.3) | async-done | bytes 2097184 | tf_op jit(solution)/shard_map/all_to_all | solution.py:25
  151.9 8.8 %all_to_all.44 = f32[2,16,128,256]{3,2,1,0:T(8,128)S(1)} all-to-all(f32[2,16,128,256]{3,2,1,0:T(8,128)S(1)} %broadcast_in_dim.10), channel_id=1, replica_groups=mesh['dp_0'=2,'dp_1'=8,'dp_2'=2,'blk'=8] {'dp_2'}, dimensions={0} | all-to-all | bytes 8388608 | tf_op jit(solution)/shard_map/all_to_all | solution.py:25
  162.6 6.8 %fusion.28 = f32[256,256]{1,0:T(8,128)S(1)} fusion(f32[2,16,128,256]{3,2,1,0:T(8,128)S(1)} %all_to_all.44), kind=kOutput, calls=%fused_computation.32 | convolution fusion | flops 3221225472 | bytes 4456448 | tf_op jit(solution)/shard_map/dot_general | solution.py:81
  169.6 11.7 %cholesky.130 = f32[128,128]{1,0:T(8,128)S(1)} custom-call(f32[128,128]{1,0:T(8,128)S(1)} %cholesky.194), custom_call_target="Cholesky" | custom-call | tf_op jit(solution)/shard_map/jit(cholesky)/cholesky | solution.py:87
  181.4 10.0 %custom-call.19 = f32[1,128,128]{1,2,0:T(8,128)S(1)} custom-call(f32[1,128,128]{2,1,0:T(8,128)S(1)} %get-tuple-element.49), custom_call_target="InvertDiagBlocksLowerTriangular" | custom-call | tf_op jit(solution)/shard_map/jit(cholesky)/cholesky | solution.py:87
  191.9 11.7 %cholesky.147 = f32[128,128]{1,0:T(8,128)S(1)} custom-call(f32[128,128]{1,0:T(8,128)S(1)} %convolution_subtract_fusion.5), custom_call_target="Cholesky" | custom-call | tf_op jit(solution)/shard_map/jit(cholesky)/cholesky | solution.py:87
  209.9 20.1 %custom-call.16 = f32[2,128,128]{1,2,0:T(8,128)S(1)} custom-call(f32[2,128,128]{2,1,0:T(8,128)S(1)} %get-tuple-element.13), custom_call_target="InvertDiagBlocksLowerTriangular" | custom-call | tf_op jit(solution)/shard_map/triangular_solve | solution.py:88
  243.0 17.9 %all_to_all.45 = f32[32,8,256]{2,1,0:T(8,128)S(1)} all-to-all(f32[32,8,256]{2,1,0:T(8,128)S(1)} %fusion.34), channel_id=1, replica_groups=mesh['dp_0'=2,'dp_1'=8,'dp_2'=2,'blk'=8] {'dp_0','dp_1','dp_2'}, dimensions={0} | all-to-all | bytes 524288 | tf_op jit(solution)/shard_map/all_to_all | solution.py:49
  260.9 6.4 %all-to-all-start = ((bf16[8,512,128]{2,1,0:T(8,128)(2,1)}), bf16[8,512,128]{2,1,0:T(8,128)(2,1)S(1)}, u32[]{:S(2)}, u32[]{:S(2)}) async-start(bf16[8,512,128]{2,1,0:T(8,128)(2,1)} %param.8), calls=%async_computation | async-start | bytes 2097152 | tf_op jit(solution)/shard_map/all_to_all | solution.py:129
  267.3 15.1 %all-to-all-done = bf16[8,512,128]{2,1,0:T(8,128)(2,1)S(1)} async-done(((bf16[8,512,128]{2,1,0:T(8,128)(2,1)}), bf16[8,512,128]{2,1,0:T(8,128)(2,1)S(1)}, u32[]{:S(2)}, u32[]{:S(2)}) %all-to-all-start) | async-done | bytes 1048608 | tf_op jit(solution)/shard_map/all_to_all | solution.py:129
  283.2 6.8 %all-to-all-start.6 = ((f32[32,8,256]{2,1,0:T(8,128)}), f32[32,8,256]{2,1,0:T(8,128)S(1)}, u32[]{:S(2)}, u32[]{:S(2)}) async-start(f32[32,8,256]{2,1,0:T(8,128)} %broadcast_in_dim.11), calls=%async_computation.6 | async-start | bytes 524288 | tf_op jit(solution)/shard_map/all_to_all | solution.py:25
  292.0 10.0 %all-to-all-done.6 = f32[32,8,256]{2,1,0:T(8,128)S(1)} async-done(((f32[32,8,256]{2,1,0:T(8,128)}), f32[32,8,256]{2,1,0:T(8,128)S(1)}, u32[]{:S(2)}, u32[]{:S(2)}) %all-to-all-start.6) | async-done | bytes 262176 | tf_op jit(solution)/shard_map/all_to_all | solution.py:25
  302.3 11.7 %cholesky.164 = f32[128,128]{1,0:T(8,128)S(1)} custom-call(f32[128,128]{1,0:T(8,128)S(1)} %cholesky.197), custom_call_target="Cholesky" | custom-call | tf_op jit(solution)/shard_map/jit(cholesky)/cholesky | solution.py:124
  314.1 9.8 %custom-call.20 = f32[1,128,128]{1,2,0:T(8,128)S(1)} custom-call(f32[1,128,128]{2,1,0:T(8,128)S(1)} %get-tuple-element.45), custom_call_target="InvertDiagBlocksLowerTriangular" | custom-call | tf_op jit(solution)/shard_map/jit(cholesky)/cholesky | solution.py:124
  324.4 11.7 %cholesky.181 = f32[128,128]{1,0:T(8,128)S(1)} custom-call(f32[128,128]{1,0:T(8,128)S(1)} %convolution_subtract_fusion.4), custom_call_target="Cholesky" | custom-call | tf_op jit(solution)/shard_map/jit(cholesky)/cholesky | solution.py:124
  342.6 19.9 %custom-call.17 = f32[2,128,128]{1,2,0:T(8,128)S(1)} custom-call(f32[2,128,128]{2,1,0:T(8,128)S(1)} %get-tuple-element.21), custom_call_target="InvertDiagBlocksLowerTriangular" | custom-call | tf_op jit(solution)/shard_map/triangular_solve | solution.py:126
  367.4 18.1 %all_to_all.46 = bf16[8,1,512,128]{3,2,1,0:T(8,128)(2,1)S(1)} all-to-all(bf16[8,1,512,128]{3,2,1,0:T(8,128)(2,1)S(1)} %fusion.41), channel_id=1, replica_groups=mesh['dp_0'=2,'dp_1'=8,'dp_2'=2,'blk'=8] {'blk'}, dimensions={0} | all-to-all | bytes 2097152 | tf_op jit(solution)/shard_map/all_to_all | solution.py:14
  (95 shorter events, 53.9 us)
Async XLA Ops:
  0.0 6.0 %copy-start = (bf16[1,4096,256]{2,1,0:T(8,128)(2,1)S(1)}, bf16[1,4096,256]{2,1,0:T(8,128)(2,1)}, u32[]{:S(2)}) copy-start(bf16[1,4096,256]{2,1,0:T(8,128)(2,1)} %param.7) | copy-start | bytes 6291460
  0.0 6.0 %copy-start.3 = (bf16[1,512,4096]{2,1,0:T(8,128)(2,1)S(1)}, bf16[1,512,4096]{2,1,0:T(8,128)(2,1)}, u32[]{:S(2)}) copy-start(bf16[1,512,4096]{2,1,0:T(8,128)(2,1)} %param.5) | copy-start | bytes 12582916
  24.3 13.0 %all-to-all-start.1 = ((f32[2,16,128,256]{2,1,3,0:T(8,128)}), f32[2,16,128,256]{2,1,3,0:T(8,128)}, u32[]{:S(2)}, u32[]{:S(2)}) async-start(f32[2,16,128,256]{2,1,3,0:T(8,128)} %bitcast.166), calls=%async_computation.1 | async-start | bytes 8388608 | tf_op jit(solution)/shard_map/all_to_all | solution.py:49
  96.6 54.8 %all-to-all-start.3 = ((f32[16,128,256]{2,1,0:T(8,128)}), f32[16,128,256]{2,1,0:T(8,128)S(1)}, u32[]{:S(2)}, u32[]{:S(2)}) async-start(f32[16,128,256]{2,1,0:T(8,128)} %broadcast_in_dim.8), calls=%async_computation.3 | async-start | bytes 4194304 | tf_op jit(solution)/shard_map/all_to_all | solution.py:25
  160.7 1.9 copy-start.2
  234.5 5.6 %copy-start.9 = (bf16[4096,128]{0,1:T(8,128)(2,1)}, bf16[4096,128]{0,1:T(8,128)(2,1)S(1)}, u32[]{:S(2)}) copy-start(bf16[4096,128]{0,1:T(8,128)(2,1)S(1)} %get-tuple-element.52) | copy-start | bytes 3145732
  234.5 6.6 %copy-start.4 = (bf16[1,512,4096]{2,1,0:T(8,128)(2,1)S(1)}, bf16[1,512,4096]{2,1,0:T(8,128)(2,1)}, u32[]{:S(2)}) copy-start(bf16[1,512,4096]{2,1,0:T(8,128)(2,1)} %param.5) | copy-start | bytes 12582916
  240.1 1.0 copy-start.5
  242.4 47.6 %copy-start.6 = (bf16[4096,128]{0,1:T(8,128)(2,1)S(1)}, bf16[4096,128]{0,1:T(8,128)(2,1)}, u32[]{:S(2)}) copy-start(bf16[4096,128]{0,1:T(8,128)(2,1)} %copy-done.5) | copy-start | bytes 3145732
  260.9 21.5 %all-to-all-start = ((bf16[8,512,128]{2,1,0:T(8,128)(2,1)}), bf16[8,512,128]{2,1,0:T(8,128)(2,1)S(1)}, u32[]{:S(2)}, u32[]{:S(2)}) async-start(bf16[8,512,128]{2,1,0:T(8,128)(2,1)} %param.8), calls=%async_computation | async-start | bytes 2097152 | tf_op jit(solution)/shard_map/all_to_all | solution.py:129
  282.5 7.6 %copy-start.8 = (bf16[8,512,128]{2,1,0:T(8,128)(2,1)}, bf16[8,512,128]{2,1,0:T(8,128)(2,1)S(1)}, u32[]{:S(2)}) copy-start(bf16[8,512,128]{2,1,0:T(8,128)(2,1)S(1)} %all-to-all-done) | copy-start | bytes 3145732
  283.2 18.7 %all-to-all-start.6 = ((f32[32,8,256]{2,1,0:T(8,128)}), f32[32,8,256]{2,1,0:T(8,128)S(1)}, u32[]{:S(2)}, u32[]{:S(2)}) async-start(f32[32,8,256]{2,1,0:T(8,128)} %broadcast_in_dim.11), calls=%async_computation.6 | async-start | bytes 524288 | tf_op jit(solution)/shard_map/all_to_all | solution.py:25
  292.0 72.7 %copy-start.7 = (bf16[4096,128]{0,1:T(8,128)(2,1)S(1)}, bf16[4096,128]{0,1:T(8,128)(2,1)}, u32[]{:S(2)}) copy-start(bf16[4096,128]{0,1:T(8,128)(2,1)} %copy-done.5) | copy-start | bytes 3145732
  364.7 21.7 %copy-start.1 = (bf16[1,4096,256]{2,1,0:T(8,128)(2,1)S(1)}, bf16[1,4096,256]{2,1,0:T(8,128)(2,1)}, u32[]{:S(2)}) copy-start(bf16[1,4096,256]{2,1,0:T(8,128)(2,1)} %param.7) | copy-start | bytes 6291460
